TPU v7x, 512 devices: a whole 4x4x16 slice. The times are simulated.
512 devices in a mesh: req: 64 (over z, x), head: 8 (over y, core).
Axes of the slice: x: 4, y: 4, z: 16, core: 2. Of those that a mesh axis runs over, the one named last changes fastest.
Arguments:
- tokens: bfloat16 [128, 1024], P('req'), may hold values from -6 to 6
- self_keys: bfloat16 [128, 512, 1024], P('req', None, 'head'), may hold values from -240 to 240
- self_values: bfloat16 [128, 512, 1024], P('req', None, 'head'), may hold values from -6 to 6
- self_len: int32 [128], P('req'), may hold values from 1 to 512, as said below
- cross_keys: bfloat16 [128, 512, 1024], P('req', None, 'head'), may hold values from -240 to 240
- cross_values: bfloat16 [128, 512, 1024], P('req', None, 'head'), may hold values from -6 to 6
- cross_len: int32 [128], P('req'), may hold values from 1 to 512, as said below
- give_slot: int32 [64], P('req'), may hold values from 0 to 1
- w_query: bfloat16 [1024, 1024], P(None, 'head'), may hold values from -0.1875 to 0.1875
- w_key: bfloat16 [1024, 1024], P(None, 'head'), may hold values from -0.1875 to 0.1875
- w_value: bfloat16 [1024, 1024], P(None, 'head'), may hold values from -0.1875 to 0.1875
- w_out: bfloat16 [1024, 1024], P('head'), may hold values from -0.1875 to 0.1875
- w_cross_query: bfloat16 [1024, 1024], P(None, 'head'), may hold values from -0.1875 to 0.1875
- w_cross_out: bfloat16 [1024, 1024], P('head'), may hold values from -0.1875 to 0.1875
- w_up: bfloat16 [1024, 4096], P(None, 'head'), may hold values from -0.1875 to 0.1875
- w_down: bfloat16 [4096, 1024], P('head'), may hold values from -0.09375 to 0.09375
- gain_self: float32 [1024], replicated, may hold values from 0.1 to 1.9
- gain_cross: float32 [1024], replicated, may hold values from 0.1 to 1.9
- gain_final: float32 [1024], replicated, may hold values from 0.1 to 1.9
Outputs:
- decoded: bfloat16 [128, 1024], P('req')
- new_keys: bfloat16 [128, 1024], P('req', 'head')
- new_values: bfloat16 [128, 1024], P('req', 'head')
- moved_keys: bfloat16 [64, 512, 1024], P('req', None, 'head')
- moved_values: bfloat16 [64, 512, 1024], P('req', None, 'head')
Inputs may be any that keep to these rules, and one draw needn't show every extreme that they name: `self_len`: each request fills at least one slot; some request fills all 512. `cross_len`: each request has at least one encoder position; some request has 512.
All inputs are finite; a program needn't handle non-finite values.
Results may differ from a plain program's by a relative error of at most 0.039.
Values may be sent and summed in bfloat16 or wider, within the bound.
No kernel may reach another device: no remote copies, remote signals or barrier semaphores. Data moves between devices by JAX's collectives and lax.ppermute only.
A program may use at most 64 MiB of HBM per device.

v0:
```python
import jax
import jax.numpy as jnp
from jax import lax
from jax.sharding import PartitionSpec as P

HEAD_DIM = 64


def passed_along(block, axis, distance):
    devices = range(lax.axis_size(axis))
    route = [((i - distance) % len(devices), i) for i in devices]
    return lax.ppermute(block, axis, route)


def layer_norm(value, gain):
    mean = jnp.mean(value, axis=-1, keepdims=True)
    centred = value - mean
    spread = jnp.mean(centred * centred, axis=-1, keepdims=True)
    return centred * lax.rsqrt(spread + 1e-05) * gain


def attend(query, keys, values, lengths, fresh_key, fresh_value):
    count, span, width = keys.shape
    heads = width // HEAD_DIM
    block = min(512, span)
    query_heads = query.reshape(count, heads, HEAD_DIM)
    steps = (jnp.max(lengths) + block - 1) // block
    places = lax.iota(jnp.int32, block)

    def score_block(index, board):
        start = index * block
        piece = keys.reshape(count, block, heads, HEAD_DIM)
        scores = jnp.einsum("qhd,qshd->qhs", query_heads, piece, preferred_element_type=jnp.float32)
        valid = (start + places)[None, None, :] < lengths[:, None, None]
        scores = jnp.where(valid, scores, -jnp.inf)
        return scores

    board = lax.fori_loop(
        0, steps, score_block, jnp.full((count, heads, span), -jnp.inf, jnp.float32)
    )
    top = jnp.max(board, axis=2)
    if fresh_key is not None:
        own = jnp.sum(
            query_heads.astype(jnp.float32)
            * fresh_key.reshape(count, heads, HEAD_DIM).astype(jnp.float32),
            axis=2,
        )
        top = jnp.maximum(top, own)
    weights_all = jnp.exp(board - top[:, :, None])
    total = jnp.sum(weights_all, axis=2)

    def mix_block(index, accum):
        start = index * block
        weights = weights_all.astype(jnp.bfloat16)
        piece = values.reshape(count, block, heads, HEAD_DIM)
        return accum + jnp.einsum(
            "qhs,qshd->qhd", weights, piece, preferred_element_type=jnp.float32
        )

    mixed = lax.fori_loop(0, steps, mix_block, jnp.zeros((count, heads, HEAD_DIM), jnp.float32))
    if fresh_key is not None:
        own_weight = jnp.exp(own - top)
        total = total + own_weight
        mixed = mixed + own_weight.astype(jnp.bfloat16).astype(jnp.float32)[
            :, :, None
        ] * fresh_value.reshape(count, heads, HEAD_DIM).astype(jnp.float32)
    return (mixed / total[:, :, None]).astype(jnp.bfloat16).reshape(count, width)


def decode_layer(
    tokens, self_keys, self_values, self_len, cross_keys, cross_values, cross_len, params
):
    (
        w_query,
        w_key,
        w_value,
        w_out,
        w_cross_query,
        w_cross_out,
        w_up,
        w_down,
        gain_self,
        gain_cross,
        gain_final,
    ) = params
    scale = HEAD_DIM ** (-0.5)
    query = (jnp.dot(tokens, w_query, preferred_element_type=jnp.float32) * scale).astype(
        jnp.bfloat16
    )
    fresh_keys = jnp.dot(tokens, w_key, preferred_element_type=jnp.float32).astype(jnp.bfloat16)
    fresh_values = jnp.dot(tokens, w_value, preferred_element_type=jnp.float32).astype(jnp.bfloat16)
    self_mixed = attend(query, self_keys, self_values, self_len, fresh_keys, fresh_values)
    self_total = lax.psum(jnp.dot(self_mixed, w_out, preferred_element_type=jnp.float32), "head")
    first = layer_norm(tokens.astype(jnp.float32) + self_total, gain_self).astype(jnp.bfloat16)
    cross_query = (
        jnp.dot(first, w_cross_query, preferred_element_type=jnp.float32) * scale
    ).astype(jnp.bfloat16)
    cross_mixed = attend(cross_query, cross_keys, cross_values, cross_len, None, None)
    cross_total = lax.psum(
        jnp.dot(cross_mixed, w_cross_out, preferred_element_type=jnp.float32), "head"
    )
    second = layer_norm(first.astype(jnp.float32) + cross_total, gain_cross).astype(jnp.bfloat16)
    hidden = jax.nn.gelu(
        jnp.dot(second, w_up, preferred_element_type=jnp.float32), approximate=False
    ).astype(jnp.bfloat16)
    ffn_total = lax.psum(jnp.dot(hidden, w_down, preferred_element_type=jnp.float32), "head")
    layer_out = layer_norm(second.astype(jnp.float32) + ffn_total, gain_final).astype(jnp.bfloat16)
    return (layer_out, fresh_keys, fresh_values)


def take_slot(array, chosen):
    return lax.dynamic_slice_in_dim(array, chosen, 1, 0)


def put_slot(array, row, chosen):
    return lax.dynamic_update_slice_in_dim(array, row, chosen, 0)


def on_device(
    tokens,
    self_keys,
    self_values,
    self_len,
    cross_keys,
    cross_values,
    cross_len,
    give_slot,
    w_query,
    w_key,
    w_value,
    w_out,
    w_cross_query,
    w_cross_out,
    w_up,
    w_down,
    gain_self,
    gain_cross,
    gain_final,
):
    params = (
        w_query,
        w_key,
        w_value,
        w_out,
        w_cross_query,
        w_cross_out,
        w_up,
        w_down,
        gain_self,
        gain_cross,
        gain_final,
    )
    chosen = give_slot[0]
    half_axis = lax.axis_size("req") // 2
    moving = passed_along(
        (
            take_slot(tokens, chosen),
            take_slot(self_keys, chosen),
            take_slot(self_values, chosen),
            take_slot(cross_keys, chosen),
            take_slot(cross_values, chosen),
        ),
        "req",
        half_axis,
    )
    arrived_len = passed_along(
        (take_slot(self_len, chosen), take_slot(cross_len, chosen)), "req", half_axis
    )
    decoded, new_keys, new_values = decode_layer(
        put_slot(tokens, moving[0], chosen),
        put_slot(self_keys, moving[1], chosen),
        put_slot(self_values, moving[2], chosen),
        put_slot(self_len, arrived_len[0], chosen),
        put_slot(cross_keys, moving[3], chosen),
        put_slot(cross_values, moving[4], chosen),
        put_slot(cross_len, arrived_len[1], chosen),
        params,
    )
    moved_keys = moving[1]
    moved_values = moving[2]
    return (decoded, new_keys, new_values, moved_keys, moved_values)


def solution(mesh):
    placed = (
        P("req", None),
        P("req", None, "head"),
        P("req", None, "head"),
        P("req"),
        P("req", None, "head"),
        P("req", None, "head"),
        P("req"),
        P("req"),
        P(None, "head"),
        P(None, "head"),
        P(None, "head"),
        P("head", None),
        P(None, "head"),
        P("head", None),
        P(None, "head"),
        P("head", None),
        P(),
        P(),
        P(),
    )
    return jax.shard_map(
        on_device,
        mesh=mesh,
        in_specs=placed,
        out_specs=(
            P("req", None),
            P("req", "head"),
            P("req", "head"),
            P("req", None, "head"),
            P("req", None, "head"),
        ),
        check_vma=False,
    )
```

profile of v0, /device:TPU:1, one launch (start us, length us, event | category | flops | bytes accessed | tf_op | source)
XLA Modules:
  0.0 135.8 jit_solution(12069132178219028557)
XLA Ops:
  0.6 0.7 copy.88
  1.4 0.7 copy.87
  2.8 0.6 dynamic_slice.22
  3.3 16.2 %collective-permute-start.1 = (s32[1]{0:T(128)}, s32[1]{0:T(128)}, u32[]{:S(2)}, u32[]{:S(2)}) collective-permute-start(s32[1]{0:T(128)} %dynamic_slice.22), channel_id=1, source_target_pairs={{256,0},{264,8},{272,16},{280,24},{288,32},{296,40},{304,48},{312,... | collective-permute-start | bytes 20 | tf_op jit(solution)/shard_map/ppermute | solution.py:12
  19.6 1.9 %collective-permute-start = (bf16[1,1024]{1,0:T(2,128)(2,1)S(1)}, bf16[1,1024]{1,0:T(2,128)(2,1)S(1)}, u32[]{:S(2)}, u32[]{:S(2)}) collective-permute-start(bf16[1,1024]{1,0:T(2,128)(2,1)S(1)} %constant_dynamic-slice_fusion.4), channel_id=1, source_target_pairs={{256,0},{264,8},{272,16},{280,24},{288,32},{296,40},{304,48},{312,... | collective-permute-start | bytes 6152 | tf_op jit(solution)/shard_map/ppermute | solution.py:12
  21.6 1.1 copy.25
  22.7 0.7 constant_dynamic-slice_fusion.3
  23.3 12.1 %collective-permute-start.2 = (bf16[1,512,128]{1,2,0:T(8,128)(2,1)}, bf16[1,512,128]{1,2,0:T(8,128)(2,1)S(1)}, u32[]{:S(2)}, u32[]{:S(2)}) collective-permute-start(bf16[1,512,128]{1,2,0:T(8,128)(2,1)} %constant_dynamic-slice_fusion.3), channel_id=1, source_target_pairs={{256,0},{264,8},{272,16},{280,24},{288,32},{296,40},{304,48},{312,... | collective-permute-start | bytes 393224 | tf_op jit(solution)/shard_map/ppermute | solution.py:12
  35.6 2.1 %collective-permute-start.3 = (bf16[1,512,128]{1,2,0:T(8,128)(2,1)S(1)}, bf16[1,512,128]{1,2,0:T(8,128)(2,1)S(1)}, u32[]{:S(2)}, u32[]{:S(2)}) collective-permute-start(bf16[1,512,128]{1,2,0:T(8,128)(2,1)S(1)} %constant_dynamic-slice_fusion.2), channel_id=1, source_target_pairs={{256,0},{264,8},{272,16},{280,24},{288,32},{296,40},{304,48},{312,... | collective-permute-start | bytes 393224 | tf_op jit(solution)/shard_map/ppermute | solution.py:12
  37.8 0.7 constant_dynamic-slice_fusion.1
  38.5 12.1 %collective-permute-start.5 = (bf16[1,512,128]{1,2,0:T(8,128)(2,1)}, bf16[1,512,128]{1,2,0:T(8,128)(2,1)S(1)}, u32[]{:S(2)}, u32[]{:S(2)}) collective-permute-start(bf16[1,512,128]{1,2,0:T(8,128)(2,1)} %constant_dynamic-slice_fusion.1), channel_id=1, source_target_pairs={{256,0},{264,8},{272,16},{280,24},{288,32},{296,40},{304,48},{312,... | collective-permute-start | bytes 393224 | tf_op jit(solution)/shard_map/ppermute | solution.py:12
  50.6 0.6 dynamic_slice.25
  51.4 2.1 %collective-permute-start.4 = (s32[1]{0:T(128)}, s32[1]{0:T(128)}, u32[]{:S(2)}, u32[]{:S(2)}) collective-permute-start(s32[1]{0:T(128)} %dynamic_slice.25), channel_id=1, source_target_pairs={{256,0},{264,8},{272,16},{280,24},{288,32},{296,40},{304,48},{312,... | collective-permute-start | bytes 20 | tf_op jit(solution)/shard_map/ppermute | solution.py:12
  53.4 0.8 dynamic_update_slice.22
  54.2 0.6 reduce_max.36
  55.5 16.9 %collective-permute-done.4 = s32[1]{0:T(128)} collective-permute-done((s32[1]{0:T(128)}, s32[1]{0:T(128)}, u32[]{:S(2)}, u32[]{:S(2)}) %collective-permute-start.4) | collective-permute-done | bytes 36 | tf_op jit(solution)/shard_map/ppermute | solution.py:12
  72.4 4.9 %collective-permute-start.6 = (bf16[1,512,128]{1,2,0:T(8,128)(2,1)S(1)}, bf16[1,512,128]{1,2,0:T(8,128)(2,1)S(1)}, u32[]{:S(2)}, u32[]{:S(2)}) collective-permute-start(bf16[1,512,128]{1,2,0:T(8,128)(2,1)S(1)} %constant_dynamic-slice_fusion), channel_id=1, source_target_pairs={{256,0},{264,8},{272,16},{280,24},{288,32},{296,40},{304,48},{312,... | collective-permute-start | bytes 393224 | tf_op jit(solution)/shard_map/ppermute | solution.py:12
  77.3 0.7 dynamic_update_slice.25
  78.1 0.6 reduce_max.38
  79.5 0.2 fusion.7
  79.7 0.2 convolution_convert_fusion.1
  79.8 0.6 copy-done.7
  80.4 0.1 convolution_convert_fusion
  80.8 0.2 copy-done.15
  81.5 0.6 broadcast.133.clone
  82.1 0.7 while.52
  82.1 0.6 broadcast_select_fusion.4
  82.8 0.9 reduce_max.37
  83.6 0.2 fusion.13
  83.8 0.2 fusion.11
  84.2 0.6 copy-done.8
  84.9 16.8 %psum.21 = f32[2,1024]{1,0:T(2,128)S(1)} all-reduce(f32[2,1024]{1,0:T(2,128)S(1)} %fusion.92), channel_id=1, replica_groups=mesh['req'=64,'head'=8] {'head'}, use_global_device_ids=true, to_apply=%region_8.9 | all-reduce | flops 2048 | bytes 16384 | tf_op jit(solution)/shard_map/psum | solution.py:93
  101.9 0.2 multiply_reduce_fusion.2
  102.2 0.1 fusion.8
  102.6 0.6 broadcast.133
  103.2 0.7 while.53
  103.3 0.6 broadcast_select_fusion.5
  103.9 0.9 fusion.6
  104.9 0.2 fusion.9
  105.2 0.6 copy-done.10
  106.0 13.7 %psum.22 = f32[2,1024]{1,0:T(2,128)S(1)} all-reduce(f32[2,1024]{1,0:T(2,128)S(1)} %fusion.94), channel_id=1, replica_groups=mesh['req'=64,'head'=8] {'head'}, use_global_device_ids=true, to_apply=%region_18.19 | all-reduce | flops 2048 | bytes 16384 | tf_op jit(solution)/shard_map/psum | solution.py:99
  119.8 0.2 multiply_reduce_fusion.1
  120.1 0.5 fusion.21
  120.6 12.6 %psum.23 = f32[2,1024]{1,0:T(2,128)S(1)} all-reduce(f32[2,1024]{1,0:T(2,128)S(1)} %fusion.21), channel_id=1, replica_groups=mesh['req'=64,'head'=8] {'head'}, use_global_device_ids=true, to_apply=%region_21.22 | all-reduce | flops 2048 | bytes 16384 | tf_op jit(solution)/shard_map/psum | solution.py:106
  133.4 0.2 multiply_reduce_fusion
  133.6 0.7 multiply_convert_fusion
  134.3 0.8 copy.32
  135.0 0.8 copy.33
  (90 shorter events, 3.1 us)
Async XLA Ops:
  0.6 119.4 %copy-start = (bf16[512,1024]{1,0:T(8,128)(2,1)S(1)}, bf16[512,1024]{1,0:T(8,128)(2,1)}, u32[]{:S(2)}) copy-start(bf16[512,1024]{1,0:T(8,128)(2,1)} %param.42) | copy-start | bytes 3145732
  1.4 0.7 copy-start.17
  3.3 48.0 %collective-permute-start.1 = (s32[1]{0:T(128)}, s32[1]{0:T(128)}, u32[]{:S(2)}, u32[]{:S(2)}) collective-permute-start(s32[1]{0:T(128)} %dynamic_slice.22), channel_id=1, source_target_pairs={{256,0},{264,8},{272,16},{280,24},{288,32},{296,40},{304,48},{312,... | collective-permute-start | bytes 20 | tf_op jit(solution)/shard_map/ppermute | solution.py:12
  19.6 59.8 %collective-permute-start = (bf16[1,1024]{1,0:T(2,128)(2,1)S(1)}, bf16[1,1024]{1,0:T(2,128)(2,1)S(1)}, u32[]{:S(2)}, u32[]{:S(2)}) collective-permute-start(bf16[1,1024]{1,0:T(2,128)(2,1)S(1)} %constant_dynamic-slice_fusion.4), channel_id=1, source_target_pairs={{256,0},{264,8},{272,16},{280,24},{288,32},{296,40},{304,48},{312,... | collective-permute-start | bytes 6152 | tf_op jit(solution)/shard_map/ppermute | solution.py:12
  22.6 12.8 %copy-start.2 = (bf16[2,512,128]{2,1,0:T(8,128)(2,1)S(1)}, bf16[2,512,128]{2,1,0:T(8,128)(2,1)}, u32[]{:S(2)}) copy-start(bf16[2,512,128]{2,1,0:T(8,128)(2,1)} %param.29) | copy-start | bytes 786436
  23.3 58.0 %collective-permute-start.2 = (bf16[1,512,128]{1,2,0:T(8,128)(2,1)}, bf16[1,512,128]{1,2,0:T(8,128)(2,1)S(1)}, u32[]{:S(2)}, u32[]{:S(2)}) collective-permute-start(bf16[1,512,128]{1,2,0:T(8,128)(2,1)} %constant_dynamic-slice_fusion.3), channel_id=1, source_target_pairs={{256,0},{264,8},{272,16},{280,24},{288,32},{296,40},{304,48},{312,... | collective-permute-start | bytes 393224 | tf_op jit(solution)/shard_map/ppermute | solution.py:12
  35.6 2.1 %copy-start.3 = (bf16[2,512,128]{2,1,0:T(8,128)(2,1)S(1)}, bf16[2,512,128]{2,1,0:T(8,128)(2,1)}, u32[]{:S(2)}) copy-start(bf16[2,512,128]{2,1,0:T(8,128)(2,1)} %param.31) | copy-start | bytes 786436
  35.6 48.2 %collective-permute-start.3 = (bf16[1,512,128]{1,2,0:T(8,128)(2,1)S(1)}, bf16[1,512,128]{1,2,0:T(8,128)(2,1)S(1)}, u32[]{:S(2)}, u32[]{:S(2)}) collective-permute-start(bf16[1,512,128]{1,2,0:T(8,128)(2,1)S(1)} %constant_dynamic-slice_fusion.2), channel_id=1, source_target_pairs={{256,0},{264,8},{272,16},{280,24},{288,32},{296,40},{304,48},{312,... | collective-permute-start | bytes 393224 | tf_op jit(solution)/shard_map/ppermute | solution.py:12
  37.8 13.3 %copy-start.4 = (bf16[2,512,128]{2,1,0:T(8,128)(2,1)S(1)}, bf16[2,512,128]{2,1,0:T(8,128)(2,1)}, u32[]{:S(2)}) copy-start(bf16[2,512,128]{2,1,0:T(8,128)(2,1)} %param.32) | copy-start | bytes 786436
  38.5 63.9 %collective-permute-start.5 = (bf16[1,512,128]{1,2,0:T(8,128)(2,1)}, bf16[1,512,128]{1,2,0:T(8,128)(2,1)S(1)}, u32[]{:S(2)}, u32[]{:S(2)}) collective-permute-start(bf16[1,512,128]{1,2,0:T(8,128)(2,1)} %constant_dynamic-slice_fusion.1), channel_id=1, source_target_pairs={{256,0},{264,8},{272,16},{280,24},{288,32},{296,40},{304,48},{312,... | collective-permute-start | bytes 393224 | tf_op jit(solution)/shard_map/ppermute | solution.py:12
  51.3 28.2 %copy-start.5 = (bf16[1024,128]{1,0:T(8,128)(2,1)S(1)}, bf16[1024,128]{1,0:T(8,128)(2,1)}, u32[]{:S(2)}) copy-start(bf16[1024,128]{1,0:T(8,128)(2,1)} %param.35) | copy-start | bytes 786436
  51.3 28.3 %copy-start.6 = (bf16[1024,128]{1,0:T(8,128)(2,1)S(1)}, bf16[1024,128]{1,0:T(8,128)(2,1)}, u32[]{:S(2)}) copy-start(bf16[1024,128]{1,0:T(8,128)(2,1)} %param.36) | copy-start | bytes 786436
  51.4 21.0 %collective-permute-start.4 = (s32[1]{0:T(128)}, s32[1]{0:T(128)}, u32[]{:S(2)}, u32[]{:S(2)}) collective-permute-start(s32[1]{0:T(128)} %dynamic_slice.25), channel_id=1, source_target_pairs={{256,0},{264,8},{272,16},{280,24},{288,32},{296,40},{304,48},{312,... | collective-permute-start | bytes 20 | tf_op jit(solution)/shard_map/ppermute | solution.py:12
  72.4 32.4 %collective-permute-start.6 = (bf16[1,512,128]{1,2,0:T(8,128)(2,1)S(1)}, bf16[1,512,128]{1,2,0:T(8,128)(2,1)S(1)}, u32[]{:S(2)}, u32[]{:S(2)}) collective-permute-start(bf16[1,512,128]{1,2,0:T(8,128)(2,1)S(1)} %constant_dynamic-slice_fusion), channel_id=1, source_target_pairs={{256,0},{264,8},{272,16},{280,24},{288,32},{296,40},{304,48},{312,... | collective-permute-start | bytes 393224 | tf_op jit(solution)/shard_map/ppermute | solution.py:12
  79.5 1.0 copy-start.7
  80.4 0.5 copy-start.15
  80.6 0.5 copy-start.16
  82.8 0.9 copy-start.11
  83.8 1.0 copy-start.8
  84.0 18.1 %copy-start.9 = (bf16[1024,128]{1,0:T(8,128)(2,1)S(1)}, bf16[1024,128]{1,0:T(8,128)(2,1)}, u32[]{:S(2)}) copy-start(bf16[1024,128]{1,0:T(8,128)(2,1)} %param.39) | copy-start | bytes 786436
  84.8 17.3 %copy-start.12 = (f32[1024]{0:T(1024)S(1)}, f32[1024]{0:T(1024)}, u32[]{:S(2)}) copy-start(f32[1024]{0:T(1024)} %param.43) | copy-start | bytes 12292
  102.1 17.9 %copy-start.1 = (bf16[1024,512]{1,0:T(8,128)(2,1)S(1)}, bf16[1024,512]{1,0:T(8,128)(2,1)}, u32[]{:S(2)}) copy-start(bf16[1024,512]{1,0:T(8,128)(2,1)} %param.41) | copy-start | bytes 3145732
  104.8 1.0 copy-start.10
  105.8 14.2 %copy-start.13 = (f32[1024]{0:T(1024)S(1)}, f32[1024]{0:T(1024)}, u32[]{:S(2)}) copy-start(f32[1024]{0:T(1024)} %param.44) | copy-start | bytes 12292
  120.1 13.5 %copy-start.14 = (f32[1024]{0:T(1024)S(1)}, f32[1024]{0:T(1024)}, u32[]{:S(2)}) copy-start(f32[1024]{0:T(1024)} %param.45) | copy-start | bytes 12292
where the time goes:
time: 136 us
  starting transfers between devices  51.3 us (38%)
  blocking collectives  43.1 us (32%)
  waiting for transfers between devices  16.9 us (12%)
  local copies, waits for them, and re-layouts  12.7 us (9%)
  other arithmetic  6.73 us (5%)
  between operations  3.02 us (2%)
  matrix products  2 us (1%)
    ppermute x7, starting transfers between devices, passed_along(): return lax.ppermute(block, axis, route)  51.3 us
    ppermute x7, waiting for transfers between devices, passed_along(): return lax.ppermute(block, axis, route)  16.9 us
    psum x1, blocking collectives, decode_layer(): lax.psum(jnp.dot(self_mixed, w_out, preferred_element_type=jnp.float32),...  16.8 us
    psum x1, blocking collectives, decode_layer(): lax.psum(jnp.dot(cross_mixed, w_cross_out, preferred_element_type=jnp.flo...  13.7 us
    psum x1, blocking collectives, decode_layer(): lax.psum(jnp.dot(hidden, w_down, preferred_element_type=jnp.float32), 'he...  12.6 us
    unnamed x45, local copies, waits for them, and re-layouts  6.63 us
  transfers between devices with their start and end apart: 7, of which 1 were waited for; matrix products, arithmetic and copies ran while one was open for 10% of the time, Pallas kernels for 0%

commit v1 on v0

--- a/solution.py
+++ b/solution.py
@@ -103,7 +103,9 @@
     hidden = jax.nn.gelu(
         jnp.dot(second, w_up, preferred_element_type=jnp.float32), approximate=False
     ).astype(jnp.bfloat16)
-    ffn_total = lax.psum(jnp.dot(hidden, w_down, preferred_element_type=jnp.float32), "head")
+    local_array = jnp.dot(hidden, w_down, preferred_element_type=jnp.float32)
+    tile_out = lax.all_gather(local_array, "head")
+    ffn_total = jnp.sum(tile_out, axis=0)
     layer_out = layer_norm(second.astype(jnp.float32) + ffn_total, gain_final).astype(jnp.bfloat16)
     return (layer_out, fresh_keys, fresh_values)
 

time: 136 us -> 137 us (level)
    all_gather x0 -> x1, blocking collectives: none -> 13.4 us  [decode_layer(): tile_out = lax.all_gather(local_array, 'head')]
    psum x1 -> x0, blocking collectives: 12.6 us -> none  [decode_layer(): lax.psum(jnp.dot(hidden, w_down, preferred_element_type=jnp.float32), 'he...]
where the time goes in v1:
time: 137 us
  starting transfers between devices  51.3 us (37%)
  blocking collectives  43.9 us (32%)
  waiting for transfers between devices  16.9 us (12%)
  local copies, waits for them, and re-layouts  12.7 us (9%)
  other arithmetic  6.76 us (5%)
  between operations  3.01 us (2%)
  matrix products  2 us (1%)
    ppermute x7, starting transfers between devices, passed_along(): return lax.ppermute(block, axis, route)  51.3 us
    ppermute x7, waiting for transfers between devices, passed_along(): return lax.ppermute(block, axis, route)  16.9 us
    psum x1, blocking collectives, decode_layer(): lax.psum(jnp.dot(self_mixed, w_out, preferred_element_type=jnp.float32),...  16.8 us
    psum x1, blocking collectives, decode_layer(): lax.psum(jnp.dot(cross_mixed, w_cross_out, preferred_element_type=jnp.flo...  13.7 us
    all_gather x1, blocking collectives, decode_layer(): tile_out = lax.all_gather(local_array, 'head')  13.4 us
    unnamed x45, local copies, waits for them, and re-layouts  6.63 us
  transfers between devices with their start and end apart: 7, of which 1 were waited for; matrix products, arithmetic and copies ran while one was open for 10% of the time, Pallas kernels for 0%

profile of v1, /device:TPU:1, one launch (start us, length us, event | category | flops | bytes accessed | tf_op | source)
XLA Modules:
  0.0 136.6 jit_solution(9257621517263688226)
XLA Ops:
  0.6 0.7 copy.99
  1.4 0.7 copy.98
  2.8 0.6 dynamic_slice.22
  3.3 16.2 %collective-permute-start.1 = (s32[1]{0:T(128)}, s32[1]{0:T(128)}, u32[]{:S(2)}, u32[]{:S(2)}) collective-permute-start(s32[1]{0:T(128)} %dynamic_slice.22), channel_id=1, source_target_pairs={{256,0},{264,8},{272,16},{280,24},{288,32},{296,40},{304,48},{312,... | collective-permute-start | bytes 20 | tf_op jit(solution)/shard_map/ppermute | solution.py:12
  19.6 1.9 %collective-permute-start = (bf16[1,1024]{1,0:T(2,128)(2,1)S(1)}, bf16[1,1024]{1,0:T(2,128)(2,1)S(1)}, u32[]{:S(2)}, u32[]{:S(2)}) collective-permute-start(bf16[1,1024]{1,0:T(2,128)(2,1)S(1)} %constant_dynamic-slice_fusion.4), channel_id=1, source_target_pairs={{256,0},{264,8},{272,16},{280,24},{288,32},{296,40},{304,48},{312,... | collective-permute-start | bytes 6152 | tf_op jit(solution)/shard_map/ppermute | solution.py:12
  21.6 1.1 copy.35
  22.7 0.7 constant_dynamic-slice_fusion.3
  23.3 12.1 %collective-permute-start.2 = (bf16[1,512,128]{1,2,0:T(8,128)(2,1)}, bf16[1,512,128]{1,2,0:T(8,128)(2,1)S(1)}, u32[]{:S(2)}, u32[]{:S(2)}) collective-permute-start(bf16[1,512,128]{1,2,0:T(8,128)(2,1)} %constant_dynamic-slice_fusion.3), channel_id=1, source_target_pairs={{256,0},{264,8},{272,16},{280,24},{288,32},{296,40},{304,48},{312,... | collective-permute-start | bytes 393224 | tf_op jit(solution)/shard_map/ppermute | solution.py:12
  35.6 2.1 %collective-permute-start.3 = (bf16[1,512,128]{1,2,0:T(8,128)(2,1)S(1)}, bf16[1,512,128]{1,2,0:T(8,128)(2,1)S(1)}, u32[]{:S(2)}, u32[]{:S(2)}) collective-permute-start(bf16[1,512,128]{1,2,0:T(8,128)(2,1)S(1)} %constant_dynamic-slice_fusion.2), channel_id=1, source_target_pairs={{256,0},{264,8},{272,16},{280,24},{288,32},{296,40},{304,48},{312,... | collective-permute-start | bytes 393224 | tf_op jit(solution)/shard_map/ppermute | solution.py:12
  37.8 0.7 constant_dynamic-slice_fusion.1
  38.5 12.1 %collective-permute-start.5 = (bf16[1,512,128]{1,2,0:T(8,128)(2,1)}, bf16[1,512,128]{1,2,0:T(8,128)(2,1)S(1)}, u32[]{:S(2)}, u32[]{:S(2)}) collective-permute-start(bf16[1,512,128]{1,2,0:T(8,128)(2,1)} %constant_dynamic-slice_fusion.1), channel_id=1, source_target_pairs={{256,0},{264,8},{272,16},{280,24},{288,32},{296,40},{304,48},{312,... | collective-permute-start | bytes 393224 | tf_op jit(solution)/shard_map/ppermute | solution.py:12
  50.6 0.6 dynamic_slice.25
  51.4 2.1 %collective-permute-start.4 = (s32[1]{0:T(128)}, s32[1]{0:T(128)}, u32[]{:S(2)}, u32[]{:S(2)}) collective-permute-start(s32[1]{0:T(128)} %dynamic_slice.25), channel_id=1, source_target_pairs={{256,0},{264,8},{272,16},{280,24},{288,32},{296,40},{304,48},{312,... | collective-permute-start | bytes 20 | tf_op jit(solution)/shard_map/ppermute | solution.py:12
  53.4 0.8 dynamic_update_slice.22
  54.2 0.6 reduce_max.36
  55.5 16.9 %collective-permute-done.4 = s32[1]{0:T(128)} collective-permute-done((s32[1]{0:T(128)}, s32[1]{0:T(128)}, u32[]{:S(2)}, u32[]{:S(2)}) %collective-permute-start.4) | collective-permute-done | bytes 36 | tf_op jit(solution)/shard_map/ppermute | solution.py:12
  72.4 4.9 %collective-permute-start.6 = (bf16[1,512,128]{1,2,0:T(8,128)(2,1)S(1)}, bf16[1,512,128]{1,2,0:T(8,128)(2,1)S(1)}, u32[]{:S(2)}, u32[]{:S(2)}) collective-permute-start(bf16[1,512,128]{1,2,0:T(8,128)(2,1)S(1)} %constant_dynamic-slice_fusion), channel_id=1, source_target_pairs={{256,0},{264,8},{272,16},{280,24},{288,32},{296,40},{304,48},{312,... | collective-permute-start | bytes 393224 | tf_op jit(solution)/shard_map/ppermute | solution.py:12
  77.3 0.7 dynamic_update_slice.25
  78.1 0.6 reduce_max.38
  79.5 0.2 fusion.7
  79.7 0.2 convolution_convert_fusion.1
  79.8 0.6 copy-done.7
  80.4 0.1 convolution_convert_fusion
  80.8 0.2 copy-done.15
  81.5 0.6 broadcast.133.clone
  82.1 0.7 while.52
  82.1 0.6 broadcast_select_fusion.4
  82.8 0.9 reduce_max.37
  83.6 0.2 fusion.13
  83.8 0.2 fusion.11
  84.2 0.6 copy-done.8
  84.9 16.8 %psum.14 = f32[2,1024]{1,0:T(2,128)S(1)} all-reduce(f32[2,1024]{1,0:T(2,128)S(1)} %fusion.91), channel_id=1, replica_groups=mesh['req'=64,'head'=8] {'head'}, use_global_device_ids=true, to_apply=%region_8.9 | all-reduce | flops 2048 | bytes 16384 | tf_op jit(solution)/shard_map/psum | solution.py:93
  101.9 0.2 multiply_reduce_fusion.2
  102.2 0.1 fusion.8
  102.6 0.6 broadcast.133
  103.2 0.7 while.53
  103.3 0.6 broadcast_select_fusion.5
  103.9 0.9 fusion.6
  104.9 0.2 fusion.9
  105.2 0.6 copy-done.10
  106.0 13.7 %psum.15 = f32[2,1024]{1,0:T(2,128)S(1)} all-reduce(f32[2,1024]{1,0:T(2,128)S(1)} %fusion.93), channel_id=1, replica_groups=mesh['req'=64,'head'=8] {'head'}, use_global_device_ids=true, to_apply=%region_18.19 | all-reduce | flops 2048 | bytes 16384 | tf_op jit(solution)/shard_map/psum | solution.py:99
  119.8 0.2 multiply_reduce_fusion.1
  120.1 0.5 convolution_bitcast_fusion
  120.6 13.4 %all-gather.1 = f32[8,2,1024]{2,1,0:T(2,128)S(1)} all-gather(f32[1,2,1024]{2,1,0:T(2,128)S(1)} %convolution_bitcast_fusion), channel_id=2, replica_groups=mesh['req'=64,'head'=8] {'head'}, dimensions={0}, use_global_device_ids=true | all-gather | bytes 73728 | tf_op jit(solution)/shard_map/all_gather | solution.py:107
  134.2 0.2 multiply_reduce_fusion
  134.4 0.7 multiply_convert_fusion
  135.0 0.8 copy.42
  135.8 0.8 copy.43
  (91 shorter events, 3.1 us)
Async XLA Ops:
  0.6 119.4 %copy-start = (bf16[512,1024]{1,0:T(8,128)(2,1)S(1)}, bf16[512,1024]{1,0:T(8,128)(2,1)}, u32[]{:S(2)}) copy-start(bf16[512,1024]{1,0:T(8,128)(2,1)} %param.42) | copy-start | bytes 3145732
  1.4 0.7 copy-start.17
  3.3 48.0 %collective-permute-start.1 = (s32[1]{0:T(128)}, s32[1]{0:T(128)}, u32[]{:S(2)}, u32[]{:S(2)}) collective-permute-start(s32[1]{0:T(128)} %dynamic_slice.22), channel_id=1, source_target_pairs={{256,0},{264,8},{272,16},{280,24},{288,32},{296,40},{304,48},{312,... | collective-permute-start | bytes 20 | tf_op jit(solution)/shard_map/ppermute | solution.py:12
  19.6 59.8 %collective-permute-start = (bf16[1,1024]{1,0:T(2,128)(2,1)S(1)}, bf16[1,1024]{1,0:T(2,128)(2,1)S(1)}, u32[]{:S(2)}, u32[]{:S(2)}) collective-permute-start(bf16[1,1024]{1,0:T(2,128)(2,1)S(1)} %constant_dynamic-slice_fusion.4), channel_id=1, source_target_pairs={{256,0},{264,8},{272,16},{280,24},{288,32},{296,40},{304,48},{312,... | collective-permute-start | bytes 6152 | tf_op jit(solution)/shard_map/ppermute | solution.py:12
  22.6 12.8 %copy-start.2 = (bf16[2,512,128]{2,1,0:T(8,128)(2,1)S(1)}, bf16[2,512,128]{2,1,0:T(8,128)(2,1)}, u32[]{:S(2)}) copy-start(bf16[2,512,128]{2,1,0:T(8,128)(2,1)} %param.29) | copy-start | bytes 786436
  23.3 58.0 %collective-permute-start.2 = (bf16[1,512,128]{1,2,0:T(8,128)(2,1)}, bf16[1,512,128]{1,2,0:T(8,128)(2,1)S(1)}, u32[]{:S(2)}, u32[]{:S(2)}) collective-permute-start(bf16[1,512,128]{1,2,0:T(8,128)(2,1)} %constant_dynamic-slice_fusion.3), channel_id=1, source_target_pairs={{256,0},{264,8},{272,16},{280,24},{288,32},{296,40},{304,48},{312,... | collective-permute-start | bytes 393224 | tf_op jit(solution)/shard_map/ppermute | solution.py:12
  35.6 2.1 %copy-start.3 = (bf16[2,512,128]{2,1,0:T(8,128)(2,1)S(1)}, bf16[2,512,128]{2,1,0:T(8,128)(2,1)}, u32[]{:S(2)}) copy-start(bf16[2,512,128]{2,1,0:T(8,128)(2,1)} %param.31) | copy-start | bytes 786436
  35.6 48.2 %collective-permute-start.3 = (bf16[1,512,128]{1,2,0:T(8,128)(2,1)S(1)}, bf16[1,512,128]{1,2,0:T(8,128)(2,1)S(1)}, u32[]{:S(2)}, u32[]{:S(2)}) collective-permute-start(bf16[1,512,128]{1,2,0:T(8,128)(2,1)S(1)} %constant_dynamic-slice_fusion.2), channel_id=1, source_target_pairs={{256,0},{264,8},{272,16},{280,24},{288,32},{296,40},{304,48},{312,... | collective-permute-start | bytes 393224 | tf_op jit(solution)/shard_map/ppermute | solution.py:12
  37.8 13.3 %copy-start.4 = (bf16[2,512,128]{2,1,0:T(8,128)(2,1)S(1)}, bf16[2,512,128]{2,1,0:T(8,128)(2,1)}, u32[]{:S(2)}) copy-start(bf16[2,512,128]{2,1,0:T(8,128)(2,1)} %param.32) | copy-start | bytes 786436
  38.5 63.9 %collective-permute-start.5 = (bf16[1,512,128]{1,2,0:T(8,128)(2,1)}, bf16[1,512,128]{1,2,0:T(8,128)(2,1)S(1)}, u32[]{:S(2)}, u32[]{:S(2)}) collective-permute-start(bf16[1,512,128]{1,2,0:T(8,128)(2,1)} %constant_dynamic-slice_fusion.1), channel_id=1, source_target_pairs={{256,0},{264,8},{272,16},{280,24},{288,32},{296,40},{304,48},{312,... | collective-permute-start | bytes 393224 | tf_op jit(solution)/shard_map/ppermute | solution.py:12
  51.3 28.2 %copy-start.5 = (bf16[1024,128]{1,0:T(8,128)(2,1)S(1)}, bf16[1024,128]{1,0:T(8,128)(2,1)}, u32[]{:S(2)}) copy-start(bf16[1024,128]{1,0:T(8,128)(2,1)} %param.35) | copy-start | bytes 786436
  51.3 28.3 %copy-start.6 = (bf16[1024,128]{1,0:T(8,128)(2,1)S(1)}, bf16[1024,128]{1,0:T(8,128)(2,1)}, u32[]{:S(2)}) copy-start(bf16[1024,128]{1,0:T(8,128)(2,1)} %param.36) | copy-start | bytes 786436
  51.4 21.0 %collective-permute-start.4 = (s32[1]{0:T(128)}, s32[1]{0:T(128)}, u32[]{:S(2)}, u32[]{:S(2)}) collective-permute-start(s32[1]{0:T(128)} %dynamic_slice.25), channel_id=1, source_target_pairs={{256,0},{264,8},{272,16},{280,24},{288,32},{296,40},{304,48},{312,... | collective-permute-start | bytes 20 | tf_op jit(solution)/shard_map/ppermute | solution.py:12
  72.4 32.4 %collective-permute-start.6 = (bf16[1,512,128]{1,2,0:T(8,128)(2,1)S(1)}, bf16[1,512,128]{1,2,0:T(8,128)(2,1)S(1)}, u32[]{:S(2)}, u32[]{:S(2)}) collective-permute-start(bf16[1,512,128]{1,2,0:T(8,128)(2,1)S(1)} %constant_dynamic-slice_fusion), channel_id=1, source_target_pairs={{256,0},{264,8},{272,16},{280,24},{288,32},{296,40},{304,48},{312,... | collective-permute-start | bytes 393224 | tf_op jit(solution)/shard_map/ppermute | solution.py:12
  79.5 1.0 copy-start.7
  80.4 0.5 copy-start.15
  80.6 0.5 copy-start.16
  82.8 0.9 copy-start.11
  83.8 1.0 copy-start.8
  84.0 18.1 %copy-start.9 = (bf16[1024,128]{1,0:T(8,128)(2,1)S(1)}, bf16[1024,128]{1,0:T(8,128)(2,1)}, u32[]{:S(2)}) copy-start(bf16[1024,128]{1,0:T(8,128)(2,1)} %param.39) | copy-start | bytes 786436
  84.8 17.3 %copy-start.12 = (f32[1024]{0:T(1024)S(1)}, f32[1024]{0:T(1024)}, u32[]{:S(2)}) copy-start(f32[1024]{0:T(1024)} %param.43) | copy-start | bytes 12292
  102.1 17.9 %copy-start.1 = (bf16[1024,512]{1,0:T(8,128)(2,1)S(1)}, bf16[1024,512]{1,0:T(8,128)(2,1)}, u32[]{:S(2)}) copy-start(bf16[1024,512]{1,0:T(8,128)(2,1)} %param.41) | copy-start | bytes 3145732
  104.8 1.0 copy-start.10
  105.8 14.2 %copy-start.13 = (f32[1024]{0:T(1024)S(1)}, f32[1024]{0:T(1024)}, u32[]{:S(2)}) copy-start(f32[1024]{0:T(1024)} %param.44) | copy-start | bytes 12292
  120.6 13.8 %copy-start.14 = (f32[1024]{0:T(1024)S(1)}, f32[1024]{0:T(1024)}, u32[]{:S(2)}) copy-start(f32[1024]{0:T(1024)} %param.45) | copy-start | bytes 12292
